TPU v7x, 128 devices: a whole 4x4x4 slice. The times are simulated.
128 devices in a mesh: ex: 8 (over z, core), sh: 16 (over y, x).
Axes of the slice: x: 4, y: 4, z: 4, core: 2. Of those that a mesh axis runs over, the one named last changes fastest.
Arguments:
- hidden_in: bfloat16 [12288, 2304], P(('ex', 'sh')), may hold values from -3 to 3
- queries: bfloat16 [12288, 2304], P(('ex', 'sh')), may hold values from -2.5 to 2.5
- new_keys: bfloat16 [12288, 2304], P(('ex', 'sh')), may hold values from -2.5 to 2.5
- new_values: bfloat16 [12288, 2304], P(('ex', 'sh')), may hold values from -6 to 6
- key_pool: bfloat16 [131072, 2304], P(('ex', 'sh')), may hold values from -2.5 to 2.5
- value_pool: bfloat16 [131072, 2304], P(('ex', 'sh')), may hold values from -6 to 6
- page_order: int32 [128, 64], P(('ex', 'sh')), may hold values from 0 to 63, each once within a row
- new_lengths: int32 [128, 4], P(('ex', 'sh')), may hold values from 1 to 48, 96 in all within a row
- context_lengths: int32 [128, 4], P(('ex', 'sh')), may hold values from 1 to 256, 512 in all within a row
- route_ids: int32 [12288, 2], P(('ex', 'sh')), may hold values from 0 to 7, all different within a row; in each aligned block of 96 rows (0 to 95, 96 to 191, ...) at most 32 rows name the same one
- norm_gain: bfloat16 [2304], replicated, may hold values from 0.25 to 1.75
- router_weight: bfloat16 [2304, 8], replicated, may hold values from -0.125 to 0.125
- gate_weight: bfloat16 [8, 2304, 5760], P('ex', None, 'sh'), may hold values from -0.125 to 0.125
- up_weight: bfloat16 [8, 2304, 5760], P('ex', None, 'sh'), may hold values from -0.125 to 0.125
- down_weight: bfloat16 [8, 5760, 2304], P('ex', 'sh'), may hold values from -0.078125 to 0.078125
- out_gain: bfloat16 [2304], replicated, may hold values from 0.25 to 1.75
Outputs:
- layer_out: bfloat16 [12288, 2304], P(('ex', 'sh'))
Inputs may be any that keep to these rules, and one draw needn't show every extreme that they name: `page_order`: each row names the pages 0 to 63 of one device's pool once each; request r owns entries r * 16 to (r+1) * 16 - 1 of its row, in order. `new_lengths`: each row sums to 96; its largest entry is 48. `context_lengths`: each row sums to 512; its largest entry is 256. `route_ids`: A row names two different experts. Among the 96 rows of one device no expert is named by more than 32 rows, and in some devices' rows one expert is named by exactly 32.
All inputs are finite; a program needn't handle non-finite values.
Results may differ from a plain program's by a relative error of at most 0.015.
Values may be sent and summed in bfloat16 or wider, within the bound.
No kernel may reach another device: no remote copies, remote signals or barrier semaphores. Data moves between devices by JAX's collectives and lax.ppermute only.
A program may use at most 128 MiB of HBM per device.

v0:
```python
import jax
import jax.numpy as jnp
from jax import lax
from jax.sharding import PartitionSpec as P

HEADS = 36
HEAD_DIM = 64
EXPERTS = 8
PAGE = 16
MOST = 32
CTX_TOTAL = 512


def rms_scale(values, gain):
    mean_square = jnp.mean(values * values, axis=-1, keepdims=True)
    return values * lax.rsqrt(mean_square + 1e-05) * gain.astype(jnp.float32)


def route_probs(normed, router_weight, route_ids):
    logits = jnp.dot(normed, router_weight, preferred_element_type=jnp.float32)
    expert_range = jnp.arange(router_weight.shape[1], dtype=jnp.int32)
    picked = jnp.sum(
        jnp.where(route_ids[:, :, None] == expert_range[None, None, :], logits[:, None, :], 0.0),
        axis=2,
    )
    raised = jnp.exp(picked)
    return raised / jnp.sum(raised, axis=1, keepdims=True)


def attend(
    hidden_rows,
    query_rows,
    key_rows,
    value_rows,
    key_store,
    value_store,
    page_row,
    new_row_lengths,
    context_row_lengths,
):
    row_count = query_rows.shape[0]
    requests = new_row_lengths.shape[0]
    table = page_row.reshape(requests, -1)
    ends = jnp.cumsum(new_row_lengths)
    row_index = jnp.arange(row_count, dtype=jnp.int32)
    owner = jnp.sum((row_index[:, None] >= ends[None, :]).astype(jnp.int32), axis=1)
    context_ends = jnp.cumsum(context_row_lengths)
    slot = jnp.arange(CTX_TOTAL, dtype=jnp.int32)
    slot_owner = jnp.sum((slot[:, None] >= context_ends[None, :]).astype(jnp.int32), axis=1)
    position = slot - (context_ends - context_row_lengths)[slot_owner]
    token = table[slot_owner, position // PAGE] * PAGE + position % PAGE
    key_store = key_store[token]
    value_store = value_store[token]
    store_mask = owner[:, None] == slot_owner[None, :]
    fresh_mask = (owner[:, None] == owner[None, :]) & (row_index[None, :] <= row_index[:, None])
    allowed = jnp.concatenate([store_mask, fresh_mask], axis=1)
    keys = jnp.concatenate([key_store, key_rows], axis=0).reshape(-1, HEADS, HEAD_DIM)
    values = jnp.concatenate([value_store, value_rows], axis=0).reshape(-1, HEADS, HEAD_DIM)
    query_heads = query_rows.reshape(row_count, HEADS, HEAD_DIM)
    scores = jnp.einsum(
        "rhd,khd->hrk", query_heads, keys, preferred_element_type=jnp.float32
    ) * HEAD_DIM ** (-0.5)
    raised = jnp.where(allowed[None, :, :], jnp.exp(scores), 0.0)
    weights = (raised / jnp.sum(raised, axis=2, keepdims=True)).astype(jnp.bfloat16)
    attended = jnp.einsum(
        "hrk,khd->rhd", weights, values, preferred_element_type=jnp.float32
    ).reshape(row_count, HEADS * HEAD_DIM)
    return hidden_rows.astype(jnp.float32) + attended


def per_device(
    hidden_in,
    queries,
    new_keys,
    new_values,
    key_pool,
    value_pool,
    page_order,
    new_lengths,
    context_lengths,
    route_ids,
    norm_gain,
    router_weight,
    gate_weight,
    up_weight,
    down_weight,
    out_gain,
):
    groups = lax.axis_size("ex")
    local_experts = gate_weight.shape[0]
    width = hidden_in.shape[1]
    row_count = hidden_in.shape[0]
    resid = attend(
        hidden_in,
        queries,
        new_keys,
        new_values,
        key_pool,
        value_pool,
        page_order[0],
        new_lengths[0],
        context_lengths[0],
    )
    normed = rms_scale(resid, norm_gain).astype(jnp.bfloat16)
    route_weights = route_probs(normed, router_weight, route_ids)
    top_count = route_ids.shape[1]
    entries = route_ids.reshape(-1)
    expert_range = jnp.arange(EXPERTS, dtype=jnp.int32)
    onehot = (entries[:, None] == expert_range[None, :]).astype(jnp.int32)
    before = jnp.cumsum(onehot, axis=0) - onehot
    slot_index = jnp.sum(before * onehot, axis=1)
    target = entries * MOST + slot_index
    entry_rows = jnp.arange(entries.shape[0], dtype=jnp.int32) // top_count
    source_row = jnp.zeros((EXPERTS * MOST,), jnp.int32).at[target].set(entry_rows)
    filled = jnp.zeros((EXPERTS * MOST,), jnp.bool_).at[target].set(True)
    outgoing = jnp.where(filled[:, None], normed[source_row], jnp.zeros((), jnp.bfloat16)).reshape(
        EXPERTS, MOST, width
    )
    arrived = lax.all_to_all(outgoing, "ex", split_axis=0, concat_axis=0, tiled=True).reshape(
        groups * MOST, width
    )
    arrived_rows = lax.all_gather(arrived, "sh", axis=0, tiled=True)
    gate_value = jnp.dot(arrived_rows, gate_weight[0], preferred_element_type=jnp.float32)
    up_value = jnp.dot(arrived_rows, up_weight[0], preferred_element_type=jnp.float32)
    hidden = (jax.nn.silu(gate_value) * up_value).astype(jnp.bfloat16)
    partial = jnp.dot(hidden, down_weight[0], preferred_element_type=jnp.float32).astype(
        jnp.bfloat16
    )
    summed = lax.psum_scatter(partial, "sh", scatter_dimension=0, tiled=True)
    returned = lax.all_to_all(
        summed.reshape(EXPERTS, MOST, width), "ex", split_axis=0, concat_axis=0, tiled=True
    )
    flat_results = returned.reshape(EXPERTS * MOST, width)
    picked = flat_results[target].reshape(row_count, top_count, width)
    mixed = resid + jnp.sum(route_weights[:, :, None] * picked.astype(jnp.float32), axis=1)
    return rms_scale(mixed, out_gain).astype(jnp.bfloat16)


def solution(mesh):
    placed = (
        P(("ex", "sh"), None),
        P(("ex", "sh"), None),
        P(("ex", "sh"), None),
        P(("ex", "sh"), None),
        P(("ex", "sh"), None),
        P(("ex", "sh"), None),
        P(("ex", "sh"), None),
        P(("ex", "sh"), None),
        P(("ex", "sh"), None),
        P(("ex", "sh"), None),
        P(),
        P(),
        P("ex", None, "sh"),
        P("ex", None, "sh"),
        P("ex", "sh", None),
        P(),
    )
    return jax.shard_map(
        per_device, mesh=mesh, in_specs=placed, out_specs=P(("ex", "sh"), None), check_vma=False
    )
```

profile of v0, /device:TPU:1, one launch (start us, length us, event | category | flops | bytes accessed | tf_op | source)
XLA Modules:
  0.0 417.7 jit_solution(15909731302938036896)
XLA Ops:
  6.5 0.0 copy-start
  6.5 0.0 all-gather.2.cloned.1.call-start
  6.5 0.8 broadcast_multiply_fusion.1
  7.4 0.8 copy.37
  8.2 0.8 reduce-window.26
  9.0 0.7 bitcast_subtract_fusion
  9.6 0.8 reduce-window.27
  10.5 0.1 convert_reduce_fusion.1
  10.6 0.5 broadcast.363
  11.1 1.3 reduce.5
  12.4 0.1 reshape_squeeze.3
  12.5 0.7 fusion.26
  13.1 0.1 convert_reduce_fusion
  13.2 0.1 fusion.10
  13.3 0.1 broadcast_compare_fusion
  13.4 2.6 fusion.17
  16.0 4.8 %gather_fusion = s32[512]{0:T(512)S(1)} fusion(s32[4,16]{1,0:T(4,128)S(1)} %reshape_squeeze.3, s32[512]{0:T(512)S(1)} %bitcast.61), kind=kCustom, calls=%fused_computation | custom fusion | bytes 8192 | tf_op jit(solution)/shard_map/gather | solution.py:51
  20.8 0.7 convert_element_type.44
  21.5 0.1 copy.36
  21.6 0.1 mul.104
  21.7 0.1 eq.72
  21.9 0.6 reduce-window.28
  22.5 0.2 slice_reduce_fusion
  22.7 0.1 add_bitcast_fusion
  22.9 1.2 scatter_custom_fusion.1
  24.1 1.4 scatter_custom_fusion
  25.5 0.1 broadcast_in_dim.46
  25.6 0.3 copy.33
  25.9 0.0 copy-start.7
  26.0 8.8 %gather_fusion.2 = bf16[512,2304]{1,0:T(8,128)(2,1)} fusion(bf16[1024,2304]{1,0:T(8,128)(2,1)} %param.20, s32[1024]{0:T(1024)S(1)} %pad_clamp_fusion.2), kind=kCustom, calls=%fused_computation.2 | custom fusion | bytes 4720640 | tf_op jit(solution)/shard_map/gather | solution.py:52
  34.7 0.0 copy-done.7
  34.7 3.4 pad_maximum_fusion.1
  38.2 5.4 %copy.32 = bf16[608,2304]{0,1:T(8,128)(2,1)} copy(bf16[608,2304]{1,0:T(8,128)(2,1)} %pad_maximum_fusion.1) | data formatting | bytes 5603328 | tf_op jit(solution)/shard_map/concatenate | solution.py:57
  43.6 8.7 %gather_fusion.1 = bf16[512,2304]{1,0:T(8,128)(2,1)} fusion(bf16[1024,2304]{1,0:T(8,128)(2,1)} %param.21, s32[1024]{0:T(1024)S(1)} %pad_clamp_fusion.2), kind=kCustom, calls=%fused_computation.1 | custom fusion | bytes 4720640 | tf_op jit(solution)/shard_map/gather | solution.py:53
  52.3 3.4 pad_maximum_fusion
  55.7 5.4 %copy.31 = bf16[608,2304]{0,1:T(8,128)(2,1)} copy(bf16[608,2304]{1,0:T(8,128)(2,1)} %pad_maximum_fusion) | data formatting | bytes 5603328 | tf_op jit(solution)/shard_map/concatenate | solution.py:58
  61.2 0.0 copy-start.5
  61.2 4.2 %fusion = (f32[36,96]{1,0:T(8,128)S(1)}, f32[36,608,96]{1,2,0:T(8,128)S(1)}) fusion(pred[96,608]{1,0:T(8,128)(4,1)S(1)} %pad_add_fusion, bf16[608,36,64]{0,2,1:T(8,128)(2,1)} %bitcast.64, bf16[96,36,64]{0,2,1:T(8,128)(2,1)S(1)} %bitcast.68), kind=kOutput, calls=%fused_computation.10 | convolution fusion | flops 275260032 | bytes 11721216 | tf_op jit(solution)/shard_map/rhd,khd->hrk/dot_general | solution.py:60
  65.4 0.0 copy-done.5
  65.4 0.0 copy-start.3
  65.4 3.5 fusion.2
  68.9 1.6 copy.34
  70.6 0.2 multiply_reduce_fusion.2
  70.8 0.2 multiply_convert_fusion.1
  71.0 2.4 gather_fusion.3
  73.4 1.4 broadcast_select_fusion
  74.8 23.2 %all_to_all.10 = bf16[8,32,2304]{2,1,0:T(8,128)(2,1)} all-to-all(bf16[8,32,2304]{2,1,0:T(8,128)(2,1)S(1)} %broadcast_select_fusion), channel_id=1, replica_groups=mesh['ex'=8,'sh'=16] {'ex'}, dimensions={0} | all-to-all | bytes 2359296 | tf_op jit(solution)/shard_map/all_to_all | solution.py:119
  98.1 0.0 all-gather.2.cloned.1.call-update
  98.1 0.3 reduce-scatter.2.cloned.1.call-start
  98.4 121.2 %all-gather.2.cloned.1.call-done = bf16[4096,2304]{1,0:T(8,128)(2,1)} async-done(((bf16[256,2304]{1,0:T(8,128)(2,1)}), bf16[4096,2304]{1,0:T(8,128)(2,1)}) %all-gather.2.cloned.1.call-update) | async-done | bytes 18874384 | tf_op jit(solution)/shard_map/all_gather | solution.py:122
  219.6 13.0 %fusion.7 = f32[4096,360]{0,1:T(8,128)} fusion(bf16[4096,2304]{1,0:T(8,128)(2,1)} %all-gather.2.cloned.1.call-done, bf16[1,2304,360]{1,2,0:T(8,128)(2,1)} %param.28), kind=kOutput, calls=%fused_computation.19 | convolution fusion | flops 6794772480 | bytes 26431488 | tf_op jit(solution)/shard_map/dot_general | solution.py:123
  232.6 25.2 %convolution_convert_fusion = bf16[4096,2304]{1,0:T(8,128)(2,1)} fusion(bf16[1,360,2304]{2,1,0:T(8,128)(2,1)S(1)} %copy-done, bf16[4096,2304]{1,0:T(8,128)(2,1)} %all-gather.2.cloned.1.call-done, f32[4096,360]{0,1:T(8,128)} %fusion.7, bf16[1,2304,360]{1,2,0:T(8,128)(2,1)} %param.29), kind=kOutput, calls=%fused_computation.7 | convolution fusion | flops 13607829504 | bytes 46964736 | tf_op jit(solution)/shard_map/dot_general | solution.py:126
  257.8 0.0 reduce-scatter.2.cloned.1.call-update
  257.8 120.5 %reduce-scatter.2.cloned.1.call-done = bf16[256,2304]{1,0:T(8,128)(2,1)} async-done(((bf16[4096,2304]{1,0:T(8,128)(2,1)}), bf16[256,2304]{1,0:T(8,128)(2,1)}) %reduce-scatter.2.cloned.1.call-update) | async-done | bytes 1179664 | tf_op jit(solution)/shard_map/reduce_scatter | solution.py:129
  378.3 5.6 %all-to-all-start.1 = ((bf16[8,32,2304]{2,1,0:T(8,128)(2,1)}), bf16[8,32,2304]{2,1,0:T(8,128)(2,1)S(1)}, u32[]{:S(2)}, u32[]{:S(2)}) async-start(bf16[8,32,2304]{2,1,0:T(8,128)(2,1)} %bitcast.66), calls=%async_computation.2 | async-start | bytes 2359296 | tf_op jit(solution)/shard_map/all_to_all | solution.py:130
  383.9 0.2 fusion.27
  384.1 0.1 select_reduce_fusion
  384.2 0.1 copy.35
  384.3 15.9 %all-to-all-done.1 = bf16[8,32,2304]{2,1,0:T(8,128)(2,1)S(1)} async-done(((bf16[8,32,2304]{2,1,0:T(8,128)(2,1)}), bf16[8,32,2304]{2,1,0:T(8,128)(2,1)S(1)}, u32[]{:S(2)}, u32[]{:S(2)}) %all-to-all-start.1) | async-done | bytes 1179680 | tf_op jit(solution)/shard_map/all_to_all | solution.py:130
  400.2 2.1 gather_fusion.4
  402.4 3.3 reshape.302
  405.6 4.0 multiply_reduce_fusion
  409.7 0.3 multiply_reduce_fusion.1
  409.9 1.0 multiply_convert_fusion
  (38 shorter events, 0.2 us)
Async XLA Ops:
  6.5 226.0 %copy-start = (bf16[1,360,2304]{2,1,0:T(8,128)(2,1)S(1)}, bf16[1,360,2304]{2,1,0:T(8,128)(2,1)}, u32[]{:S(2)}) copy-start(bf16[1,360,2304]{2,1,0:T(8,128)(2,1)} %param.30) | copy-start | bytes 4976644
  6.5 19.1 %copy-start.6 = (bf16[96,2304]{1,0:T(8,128)(2,1)S(1)}, bf16[96,2304]{1,0:T(8,128)(2,1)}, u32[]{:S(2)}) copy-start(bf16[96,2304]{1,0:T(8,128)(2,1)} %param.17) | copy-start | bytes 1327108
  6.5 213.0 %all-gather.2.cloned.1.call-start = ((), (), s32[]{:S(2)}) async-start(), calls=%async_computation.3 | async-start | bytes 20054016 | tf_op jit(solution)/shard_map/all_gather | solution.py:122
  25.9 8.8 %copy-start.7 = (bf16[96,2304]{1,0:T(8,128)(2,1)S(1)}, bf16[96,2304]{1,0:T(8,128)(2,1)}, u32[]{:S(2)}) copy-start(bf16[96,2304]{1,0:T(8,128)(2,1)} %param.18) | copy-start | bytes 1327108
  43.6 8.7 %copy-start.8 = (bf16[96,2304]{1,0:T(8,128)(2,1)S(1)}, bf16[96,2304]{1,0:T(8,128)(2,1)}, u32[]{:S(2)}) copy-start(bf16[96,2304]{1,0:T(8,128)(2,1)} %param.19) | copy-start | bytes 1327108
  61.2 4.2 %copy-start.5 = (bf16[608,2304]{0,1:T(8,128)(2,1)S(1)}, bf16[608,2304]{0,1:T(8,128)(2,1)}, u32[]{:S(2)}) copy-start(bf16[608,2304]{0,1:T(8,128)(2,1)} %copy.31) | copy-start | bytes 8404996
  65.4 5.1 %copy-start.3 = (bf16[96,2304]{1,0:T(8,128)(2,1)S(1)}, bf16[96,2304]{1,0:T(8,128)(2,1)}, u32[]{:S(2)}) copy-start(bf16[96,2304]{1,0:T(8,128)(2,1)} %param.16) | copy-start | bytes 1327108
  70.6 2.8 copy-start.1
  98.1 280.2 %reduce-scatter.2.cloned.1.call-start = ((), (), s32[]{:S(2)}) async-start(), calls=%async_computation.4 | async-start | bytes 20054016 | tf_op jit(solution)/shard_map/reduce_scatter | solution.py:129
  257.8 126.1 %copy-start.11 = (bf16[2304]{0:T(1024)(128)(2,1)S(1)}, bf16[2304]{0:T(1024)(128)(2,1)}, u32[]{:S(2)}) copy-start(bf16[2304]{0:T(1024)(128)(2,1)} %param.31) | copy-start | bytes 13828
  257.8 126.1 %copy-start.9 = (bf16[2304,8]{0,1:T(8,128)(2,1)S(1)}, bf16[2304,8]{0,1:T(8,128)(2,1)}, u32[]{:S(2)}) copy-start(bf16[2304,8]{0,1:T(8,128)(2,1)} %param.27) | copy-start | bytes 110596
  257.8 126.3 %copy-start.10 = (s32[96,2]{0,1:T(2,128)S(1)}, s32[96,2]{0,1:T(2,128)}, u32[]{:S(2)}) copy-start(s32[96,2]{0,1:T(2,128)} %param.25) | copy-start | bytes 2308
  378.3 21.9 %all-to-all-start.1 = ((bf16[8,32,2304]{2,1,0:T(8,128)(2,1)}), bf16[8,32,2304]{2,1,0:T(8,128)(2,1)S(1)}, u32[]{:S(2)}, u32[]{:S(2)}) async-start(bf16[8,32,2304]{2,1,0:T(8,128)(2,1)} %bitcast.66), calls=%async_computation.2 | async-start | bytes 2359296 | tf_op jit(solution)/shard_map/all_to_all | solution.py:130
  402.4 7.3 %copy-start.2 = (f32[96,2304]{1,0:T(8,128)S(1)}, f32[96,2304]{1,0:T(8,128)}, u32[]{:S(2)}) copy-start(f32[96,2304]{1,0:T(8,128)} %copy-done.1) | copy-start | bytes 2654212
  402.4 7.3 %copy-start.4 = (bf16[96,2304]{1,0:T(8,128)(2,1)S(1)}, bf16[96,2304]{1,0:T(8,128)(2,1)}, u32[]{:S(2)}) copy-start(bf16[96,2304]{1,0:T(8,128)(2,1)} %param.16) | copy-start | bytes 1327108
Sparse Core Ops, SparseCore 0:
  98.2 121.3 all-gather.1
  257.9 120.3 reduce-scatter.1
where the time goes:
time: 418 us
  waiting for transfers between devices  258 us (62%)
  local copies, waits for them, and re-layouts  48.4 us (12%)
  matrix products  46.1 us (11%)
  blocking collectives  23.2 us (6%)
  other arithmetic  22.9 us (5%)
  between operations  13.7 us (3%)
  starting transfers between devices  5.84 us (1%)
    all_gather x1, waiting for transfers between devices, per_device(): arrived_rows = lax.all_gather(arrived, 'sh', axis=0, tiled=True)  121 us
    reduce_scatter x1, waiting for transfers between devices, per_device(): summed = lax.psum_scatter(partial, 'sh', scatter_dimension=0, tiled=True)  121 us
    dot_general x1, matrix products, per_device(): jnp.dot(hidden, down_weight[0], preferred_element_type=jnp.float32)  25.2 us
    all_to_all x1, blocking collectives, per_device(): lax.all_to_all(outgoing, 'ex', split_axis=0, concat_axis=0, tiled=True)  23.2 us
    all_to_all x1, waiting for transfers between devices, per_device(): lax.all_to_all(summed.reshape(EXPERTS, MOST, width), 'ex', split_axis=0,...  15.9 us
    dot_general x1, matrix products, per_device(): jnp.dot(arrived_rows, gate_weight[0], preferred_element_type=jnp.float32)  13 us
    gather x1, local copies, waits for them, and re-layouts, attend(): key_store = key_store[token]  8.78 us
    gather x1, local copies, waits for them, and re-layouts, attend(): value_store = value_store[token]  8.73 us
  transfers between devices with their start and end apart: 3, of which 3 were waited for; matrix products, arithmetic and copies ran while one was open for 0% of the time, Pallas kernels for 0%

commit v1 on v0

--- a/solution.py
+++ b/solution.py
@@ -9,6 +9,28 @@
 PAGE = 16
 MOST = 32
 CTX_TOTAL = 512
+
+
+def cut_along(shard, dim, devices):
+    before, after = (shard.shape[:dim], shard.shape[dim + 1 :])
+    return jnp.moveaxis(shard.reshape(*before, devices, -1, *after), dim, 0)
+
+
+def laid_out(blocks, dim):
+    blocks = jnp.moveaxis(blocks, 0, dim)
+    dims = blocks.shape
+    return blocks.reshape(*dims[:dim], dims[dim] * dims[dim + 1], *dims[dim + 2 :])
+
+
+def swapped_with_each(value, axis, split_dim, concat_dim):
+    peers, index = (lax.axis_size(axis), lax.axis_index(axis))
+    parts = cut_along(value, split_dim, peers)
+    done = [parts[index]]
+    for step in range(1, peers):
+        sent = parts[index ^ step]
+        done.append(lax.ppermute(sent, axis, [(i, i ^ step) for i in range(peers)]))
+    parts = jnp.stack(done)[index ^ jnp.arange(peers)]
+    return laid_out(parts, concat_dim)
 
 
 def rms_scale(values, gain):
@@ -127,9 +149,7 @@
         jnp.bfloat16
     )
     summed = lax.psum_scatter(partial, "sh", scatter_dimension=0, tiled=True)
-    returned = lax.all_to_all(
-        summed.reshape(EXPERTS, MOST, width), "ex", split_axis=0, concat_axis=0, tiled=True
-    )
+    returned = swapped_with_each(summed.reshape(EXPERTS, MOST, width), "ex", 0, 0)
     flat_results = returned.reshape(EXPERTS * MOST, width)
     picked = flat_results[target].reshape(row_count, top_count, width)
     mixed = resid + jnp.sum(route_weights[:, :, None] * picked.astype(jnp.float32), axis=1)

time: 418 us -> 425 us (1.017)
  local copies, waits for them, and re-layouts: 48.4 us -> 55 us
    all_to_all x1 -> x0, waiting for transfers between devices: 15.9 us -> none  [per_device(): lax.all_to_all(summed.reshape(EXPERTS, MOST, width), 'ex', split_axis=0,...]
    ppermute x0 -> x7, waiting for transfers between devices: none -> 15.3 us  [swapped_with_each(): done.append(lax.ppermute(sent, axis, [(i, i ^ step) for i in range(peers)]))]
    ppermute x0 -> x7, starting transfers between devices: none -> 7.87 us  [swapped_with_each(): done.append(lax.ppermute(sent, axis, [(i, i ^ step) for i in range(peers)]))]
    all_to_all x1 -> x0, starting transfers between devices: 5.57 us -> none  [per_device(): lax.all_to_all(summed.reshape(EXPERTS, MOST, width), 'ex', split_axis=0,...]
  transfers between devices with their start and end apart: 3 -> 9, of which waited for: 3 -> 4; matrix products, arithmetic and copies ran while one was open for 0% -> 0% of each run, Pallas kernels for 0% -> 0%
where the time goes in v1:
time: 425 us
  waiting for transfers between devices  256 us (60%)
  local copies, waits for them, and re-layouts  55 us (13%)
  matrix products  46.1 us (11%)
  blocking collectives  23.2 us (5%)
  other arithmetic  22.3 us (5%)
  between operations  13.8 us (3%)
  starting transfers between devices  8.14 us (2%)
    all_gather x1, waiting for transfers between devices, per_device(): arrived_rows = lax.all_gather(arrived, 'sh', axis=0, tiled=True)  121 us
    reduce_scatter x1, waiting for transfers between devices, per_device(): summed = lax.psum_scatter(partial, 'sh', scatter_dimension=0, tiled=True)  120 us
    dot_general x1, matrix products, per_device(): jnp.dot(hidden, down_weight[0], preferred_element_type=jnp.float32)  25.2 us
    all_to_all x1, blocking collectives, per_device(): lax.all_to_all(outgoing, 'ex', split_axis=0, concat_axis=0, tiled=True)  23.2 us
    ppermute x7, waiting for transfers between devices, swapped_with_each(): done.append(lax.ppermute(sent, axis, [(i, i ^ step) for i in range(peers)]))  15.3 us
    dot_general x1, matrix products, per_device(): jnp.dot(arrived_rows, gate_weight[0], preferred_element_type=jnp.float32)  13 us
    gather x1, local copies, waits for them, and re-layouts, attend(): key_store = key_store[token]  8.78 us
    gather x1, local copies, waits for them, and re-layouts, attend(): value_store = value_store[token]  8.73 us
  transfers between devices with their start and end apart: 9, of which 4 were waited for; matrix products, arithmetic and copies ran while one was open for 0% of the time, Pallas kernels for 0%

profile of v1, /device:TPU:1, one launch (start us, length us, event | category | flops | bytes accessed | tf_op | source)
XLA Modules:
  0.0 424.6 jit_solution(11209382772405830494)
XLA Ops:
  6.6 0.8 broadcast_multiply_fusion.1
  7.4 0.8 copy.37
  8.2 0.8 reduce-window.26
  9.0 0.7 bitcast_subtract_fusion
  9.6 0.8 reduce-window.27
  10.5 0.1 convert_reduce_fusion.1
  10.6 0.5 broadcast.406
  11.1 1.3 reduce.5
  12.4 0.1 reshape_squeeze.3
  12.5 0.7 fusion.27
  13.1 0.1 convert_reduce_fusion
  13.2 0.1 fusion.10
  13.3 0.1 broadcast_compare_fusion
  13.4 2.6 fusion.17
  16.0 4.8 %gather_fusion = s32[512]{0:T(512)S(1)} fusion(s32[4,16]{1,0:T(4,128)S(1)} %reshape_squeeze.3, s32[512]{0:T(512)S(1)} %bitcast.92), kind=kCustom, calls=%fused_computation | custom fusion | bytes 8192 | tf_op jit(solution)/shard_map/gather | solution.py:73
  20.8 0.1 copy.36
  20.9 0.1 mul.104
  21.1 0.1 eq.72
  21.2 0.6 reduce-window.28
  21.8 0.2 slice_reduce_fusion
  22.2 1.2 scatter_custom_fusion.1
  23.4 1.4 scatter_custom_fusion
  24.9 0.1 broadcast_in_dim.46
  25.0 0.3 copy.33
  25.3 8.8 %gather_fusion.2 = bf16[512,2304]{1,0:T(8,128)(2,1)} fusion(bf16[1024,2304]{1,0:T(8,128)(2,1)} %param.20, s32[1024]{0:T(1024)S(1)} %pad_clamp_fusion.3), kind=kCustom, calls=%fused_computation.2 | custom fusion | bytes 4720640 | tf_op jit(solution)/shard_map/gather | solution.py:74
  34.1 3.4 pad_maximum_fusion.1
  37.5 5.4 %copy.32 = bf16[608,2304]{0,1:T(8,128)(2,1)} copy(bf16[608,2304]{1,0:T(8,128)(2,1)} %pad_maximum_fusion.1) | data formatting | bytes 5603328 | tf_op jit(solution)/shard_map/concatenate | solution.py:79
  42.9 8.7 %gather_fusion.1 = bf16[512,2304]{1,0:T(8,128)(2,1)} fusion(bf16[1024,2304]{1,0:T(8,128)(2,1)} %param.21, s32[1024]{0:T(1024)S(1)} %pad_clamp_fusion.3), kind=kCustom, calls=%fused_computation.1 | custom fusion | bytes 4720640 | tf_op jit(solution)/shard_map/gather | solution.py:75
  51.6 3.4 pad_maximum_fusion
  55.1 5.4 %copy.31 = bf16[608,2304]{0,1:T(8,128)(2,1)} copy(bf16[608,2304]{1,0:T(8,128)(2,1)} %pad_maximum_fusion) | data formatting | bytes 5603328 | tf_op jit(solution)/shard_map/concatenate | solution.py:80
  60.5 4.2 fusion
  64.8 3.5 fusion.2
  68.3 1.7 copy.34
  70.0 0.2 multiply_reduce_fusion.2
  70.2 0.2 multiply_convert_fusion.1
  70.3 2.4 gather_fusion.3
  72.8 1.4 broadcast_select_fusion
  74.2 23.2 %all_to_all.5 = bf16[8,32,2304]{2,1,0:T(8,128)(2,1)} all-to-all(bf16[8,32,2304]{2,1,0:T(8,128)(2,1)S(1)} %broadcast_select_fusion), channel_id=1, replica_groups=mesh['ex'=8,'sh'=16] {'ex'}, dimensions={0} | all-to-all | bytes 2359296 | tf_op jit(solution)/shard_map/all_to_all | solution.py:141
  97.5 0.3 reduce-scatter.2.cloned.1.call-start
  97.7 121.2 %all-gather.2.cloned.1.call-done = bf16[4096,2304]{1,0:T(8,128)(2,1)} async-done(((bf16[256,2304]{1,0:T(8,128)(2,1)}), bf16[4096,2304]{1,0:T(8,128)(2,1)}) %all-gather.2.cloned.1.call-update) | async-done | bytes 18874384 | tf_op jit(solution)/shard_map/all_gather | solution.py:144
  218.9 13.0 %fusion.7 = f32[4096,360]{0,1:T(8,128)} fusion(bf16[4096,2304]{1,0:T(8,128)(2,1)} %all-gather.2.cloned.1.call-done, bf16[1,2304,360]{1,2,0:T(8,128)(2,1)} %param.28), kind=kOutput, calls=%fused_computation.20 | convolution fusion | flops 6794772480 | bytes 26431488 | tf_op jit(solution)/shard_map/dot_general | solution.py:145
  231.9 25.2 %convolution_convert_fusion = bf16[4096,2304]{1,0:T(8,128)(2,1)} fusion(bf16[1,360,2304]{2,1,0:T(8,128)(2,1)S(1)} %copy-done, bf16[4096,2304]{1,0:T(8,128)(2,1)} %all-gather.2.cloned.1.call-done, f32[4096,360]{0,1:T(8,128)} %fusion.7, bf16[1,2304,360]{1,2,0:T(8,128)(2,1)} %param.29), kind=kOutput, calls=%fused_computation.8 | convolution fusion | flops 13607829504 | bytes 46964736 | tf_op jit(solution)/shard_map/dot_general | solution.py:148
  257.2 0.7 copy-done.8
  257.9 0.2 fusion.28
  258.2 119.5 %reduce-scatter.2.cloned.1.call-done = bf16[256,2304]{1,0:T(8,128)(2,1)} async-done(((bf16[4096,2304]{1,0:T(8,128)(2,1)}), bf16[256,2304]{1,0:T(8,128)(2,1)}) %reduce-scatter.2.cloned.1.call-update) | async-done | bytes 1179664 | tf_op jit(solution)/shard_map/reduce_scatter | solution.py:151
  377.7 2.1 dynamic-slice_bitcast_fusion
  379.8 1.1 collective-permute-start
  381.0 0.1 copy.35
  381.1 2.6 collective-permute-start.6
  383.7 0.2 collective-permute-start.5
  383.9 2.2 collective-permute-start.4
  386.1 1.3 collective-permute-start.3
  387.4 0.3 collective-permute-start.1
  387.6 0.9 bitcast_dynamic-update-slice_fusion.6
  388.6 9.7 %collective-permute-done.1 = bf16[1,32,2304]{2,1,0:T(8,128)(2,1)S(1)} collective-permute-done((bf16[1,32,2304]{2,1,0:T(8,128)(2,1)}, bf16[1,32,2304]{2,1,0:T(8,128)(2,1)S(1)}, u32[]{:S(2)}, u32[]{:S(2)}) %collective-permute-start.1) | collective-permute-done | bytes 147488 | tf_op jit(solution)/shard_map/ppermute | solution.py:31
  398.2 0.2 collective-permute-start.2
  398.4 5.7 %collective-permute-done.2 = bf16[1,32,2304]{2,1,0:T(8,128)(2,1)S(1)} collective-permute-done((bf16[1,32,2304]{2,1,0:T(8,128)(2,1)S(1)}, bf16[1,32,2304]{2,1,0:T(8,128)(2,1)S(1)}, u32[]{:S(2)}, u32[]{:S(2)}) %collective-permute-start.2) | collective-permute-done | bytes 147488 | tf_op jit(solution)/shard_map/ppermute | solution.py:31
  404.2 1.0 copy-done.4
  405.2 1.9 gather_fusion.4
  407.1 2.1 gather_fusion.5
  409.3 3.2 reshape.310
  412.4 4.1 multiply_reduce_fusion
  416.5 0.3 multiply_reduce_fusion.1
  416.8 1.0 multiply_convert_fusion
  (60 shorter events, 0.5 us)
Async XLA Ops:
  6.5 225.4 %copy-start = (bf16[1,360,2304]{2,1,0:T(8,128)(2,1)S(1)}, bf16[1,360,2304]{2,1,0:T(8,128)(2,1)}, u32[]{:S(2)}) copy-start(bf16[1,360,2304]{2,1,0:T(8,128)(2,1)} %param.30) | copy-start | bytes 4976644
  6.5 14.3 %copy-start.10 = (bf16[2304]{0:T(1024)(128)(2,1)S(1)}, bf16[2304]{0:T(1024)(128)(2,1)}, u32[]{:S(2)}) copy-start(bf16[2304]{0:T(1024)(128)(2,1)} %param.26) | copy-start | bytes 13828
  6.5 18.4 %copy-start.5 = (bf16[96,2304]{1,0:T(8,128)(2,1)S(1)}, bf16[96,2304]{1,0:T(8,128)(2,1)}, u32[]{:S(2)}) copy-start(bf16[96,2304]{1,0:T(8,128)(2,1)} %param.17) | copy-start | bytes 1327108
  6.5 212.4 %all-gather.2.cloned.1.call-start = ((), (), s32[]{:S(2)}) async-start(), calls=%async_computation.2 | async-start | bytes 20054016 | tf_op jit(solution)/shard_map/all_gather | solution.py:144
  25.3 8.8 %copy-start.6 = (bf16[96,2304]{1,0:T(8,128)(2,1)S(1)}, bf16[96,2304]{1,0:T(8,128)(2,1)}, u32[]{:S(2)}) copy-start(bf16[96,2304]{1,0:T(8,128)(2,1)} %param.18) | copy-start | bytes 1327108
  42.9 8.7 %copy-start.7 = (bf16[96,2304]{1,0:T(8,128)(2,1)S(1)}, bf16[96,2304]{1,0:T(8,128)(2,1)}, u32[]{:S(2)}) copy-start(bf16[96,2304]{1,0:T(8,128)(2,1)} %param.19) | copy-start | bytes 1327108
  60.5 4.2 copy-start.3
  68.3 1.7 copy-start.2
  97.5 280.2 %reduce-scatter.2.cloned.1.call-start = ((), (), s32[]{:S(2)}) async-start(), calls=%async_computation.3 | async-start | bytes 20054016 | tf_op jit(solution)/shard_map/reduce_scatter | solution.py:151
  257.1 0.8 copy-start.8
  257.1 1.0 copy-start.9
  257.1 123.8 %copy-start.11 = (bf16[2304]{0:T(1024)(128)(2,1)S(1)}, bf16[2304]{0:T(1024)(128)(2,1)}, u32[]{:S(2)}) copy-start(bf16[2304]{0:T(1024)(128)(2,1)} %param.31) | copy-start | bytes 13828
  379.8 7.6 %collective-permute-start = (bf16[1,32,2304]{2,1,0:T(8,128)(2,1)}, bf16[1,32,2304]{2,1,0:T(8,128)(2,1)}, u32[]{:S(2)}, u32[]{:S(2)}) collective-permute-start(bf16[1,32,2304]{2,1,0:T(8,128)(2,1)} %get-tuple-element.13), channel_id=1, source_target_pairs={{0,16},{16,0},{32,48},{48,32},{64,80},{80,64},{96,112},{112,96},{1... | collective-permute-start | bytes 442376 | tf_op jit(solution)/shard_map/ppermute | solution.py:31
  381.1 23.1 %collective-permute-start.6 = (bf16[1,32,2304]{2,1,0:T(8,128)(2,1)S(1)}, bf16[1,32,2304]{2,1,0:T(8,128)(2,1)S(1)}, u32[]{:S(2)}, u32[]{:S(2)}) collective-permute-start(bf16[1,32,2304]{2,1,0:T(8,128)(2,1)S(1)} %get-tuple-element.7), channel_id=1, source_target_pairs={{0,112},{16,96},{32,80},{48,64},{64,48},{80,32},{96,16},{112,0},{1... | collective-permute-start | bytes 442376 | tf_op jit(solution)/shard_map/ppermute | solution.py:31
  383.7 20.4 %collective-permute-start.5 = (bf16[1,32,2304]{2,1,0:T(8,128)(2,1)S(1)}, bf16[1,32,2304]{2,1,0:T(8,128)(2,1)S(1)}, u32[]{:S(2)}, u32[]{:S(2)}) collective-permute-start(bf16[1,32,2304]{2,1,0:T(8,128)(2,1)S(1)} %get-tuple-element.8), channel_id=1, source_target_pairs={{0,96},{16,112},{32,64},{48,80},{64,32},{80,48},{96,0},{112,16},{1... | collective-permute-start | bytes 442376 | tf_op jit(solution)/shard_map/ppermute | solution.py:31
  383.9 20.2 %collective-permute-start.4 = (bf16[1,32,2304]{2,1,0:T(8,128)(2,1)S(1)}, bf16[1,32,2304]{2,1,0:T(8,128)(2,1)S(1)}, u32[]{:S(2)}, u32[]{:S(2)}) collective-permute-start(bf16[1,32,2304]{2,1,0:T(8,128)(2,1)S(1)} %get-tuple-element.9), channel_id=1, source_target_pairs={{0,80},{16,64},{32,112},{48,96},{64,16},{80,0},{96,48},{112,32},{1... | collective-permute-start | bytes 442376 | tf_op jit(solution)/shard_map/ppermute | solution.py:31
  386.1 18.0 %collective-permute-start.3 = (bf16[1,32,2304]{2,1,0:T(8,128)(2,1)S(1)}, bf16[1,32,2304]{2,1,0:T(8,128)(2,1)S(1)}, u32[]{:S(2)}, u32[]{:S(2)}) collective-permute-start(bf16[1,32,2304]{2,1,0:T(8,128)(2,1)S(1)} %get-tuple-element.10), channel_id=1, source_target_pairs={{0,64},{16,80},{32,96},{48,112},{64,0},{80,16},{96,32},{112,48},{1... | collective-permute-start | bytes 442376 | tf_op jit(solution)/shard_map/ppermute | solution.py:31
  387.4 10.9 %collective-permute-start.1 = (bf16[1,32,2304]{2,1,0:T(8,128)(2,1)}, bf16[1,32,2304]{2,1,0:T(8,128)(2,1)S(1)}, u32[]{:S(2)}, u32[]{:S(2)}) collective-permute-start(bf16[1,32,2304]{2,1,0:T(8,128)(2,1)} %get-tuple-element.12), channel_id=1, source_target_pairs={{0,32},{16,48},{32,0},{48,16},{64,96},{80,112},{96,64},{112,80},{1... | collective-permute-start | bytes 442376 | tf_op jit(solution)/shard_map/ppermute | solution.py:31
  398.2 5.9 %collective-permute-start.2 = (bf16[1,32,2304]{2,1,0:T(8,128)(2,1)S(1)}, bf16[1,32,2304]{2,1,0:T(8,128)(2,1)S(1)}, u32[]{:S(2)}, u32[]{:S(2)}) collective-permute-start(bf16[1,32,2304]{2,1,0:T(8,128)(2,1)S(1)} %get-tuple-element.11), channel_id=1, source_target_pairs={{0,48},{16,32},{32,16},{48,0},{64,112},{80,96},{96,80},{112,64},{1... | collective-permute-start | bytes 442376 | tf_op jit(solution)/shard_map/ppermute | solution.py:31
  404.2 1.0 copy-start.4
  412.4 5.4 %copy-start.1 = (bf16[1,360,2304]{2,1,0:T(8,128)(2,1)S(1)}, bf16[1,360,2304]{2,1,0:T(8,128)(2,1)}, u32[]{:S(2)}) copy-start(bf16[1,360,2304]{2,1,0:T(8,128)(2,1)} %param.30) | copy-start | bytes 4976644
Sparse Core Ops, SparseCore 0:
  97.6 121.3 all-gather.1
  257.3 120.3 reduce-scatter.1
